TPU v7x, 256 devices: a whole 4x4x8 slice. The times are simulated.
256 devices in a mesh: rep: 8 (over x, core), seq: 32 (over y, z).
Axes of the slice: x: 4, y: 4, z: 8, core: 2. Of those that a mesh axis runs over, the one named last changes fastest.
Arguments:
- tokens: bfloat16 [16, 256, 32, 1024], P('rep', 'seq'), may hold values from -250 to 250
- cotangent: bfloat16 [16, 256, 32, 1024], P('rep', 'seq'), may hold values from -6 to 6
- clip_counts: int32 [8], P('rep'), may hold values from 1 to 2, as said below
- windows: int32 [16, 4, 3], P('rep'), may hold values from 0 to 3, as said below
- window_counts: int32 [16, 4], P('rep'), may hold values from 1 to 3, as said below
- norm_gain: float32 [1024], replicated, may hold values from 0.5 to 4
- norm_bias: float32 [1024], replicated, may hold values from -3 to 3
- qkv_weight: bfloat16 [1024, 3072], replicated, may hold values from -0.5 to 0.5
- out_weight: bfloat16 [1024, 1024], replicated, may hold values from -0.1875 to 0.1875
Outputs:
- grad_input: bfloat16 [16, 256, 32, 1024], P('rep', 'seq')
- grad_qkv_weight: float32 [1024, 3072], P('seq')
- grad_out_weight: float32 [1024, 1024], P('seq')
- grad_gain: float32 [1024], P('seq')
- grad_bias: float32 [1024], P('seq')
Inputs may be any that keep to these rules, and one draw needn't show every extreme that they name: `clip_counts`: slots of a group at or past its count hold no clip; some group is full. `windows`: the first entry of each list is the window itself; the entries of a list are distinct. `window_counts`: some window of every clip uses all 3 entries.
All inputs are finite; a program needn't handle non-finite values.
Results may differ from a plain program's by a relative error of at most 0.025.
The roundings to bfloat16 on the way count: a program that leaves them out, or rounds other values in their place, can miss the bound.
Values may be sent and summed in bfloat16 or wider, within the bound.
No kernel may reach another device: no remote copies, remote signals or barrier semaphores. Data moves between devices by JAX's collectives and lax.ppermute only.
A program may use at most 128 MiB of HBM per device.

v0:
```python
from functools import partial
import math

import jax
import jax.numpy as jnp
from jax import lax
from jax.sharding import Mesh, PartitionSpec as P
import numpy as np

D = 1024
HEADS = 16
HEAD_DIM = 64
WIN = 64
MAXW = 3
NWIN = 4


EPSILON = 1e-05


def frame_mask(window_list, list_count, frame_count):
    used_slot = jnp.arange(MAXW)[None, :] < list_count[:, None]
    listed = (window_list[:, :, None] == jnp.arange(NWIN)[None, None, :]) & used_slot[:, :, None]
    allowed = jnp.any(listed, axis=1).astype(jnp.float32)
    member = (jnp.arange(frame_count)[:, None] // WIN == jnp.arange(NWIN)[None, :]).astype(
        jnp.float32
    )
    return jnp.dot(jnp.dot(member, allowed), member.T) > 0.5


def local(
    tokens,
    cotangent,
    clip_counts,
    windows,
    window_counts,
    norm_gain,
    norm_bias,
    qkv_weight,
    out_weight,
):
    seq_size = lax.axis_size(("y", "z"))
    rep_size = lax.axis_size(("x", "core"))
    clip_count = tokens.shape[0]
    live_slot = jnp.arange(clip_count) < clip_counts[0]
    grad_live = jnp.where(live_slot[:, None, None, None], cotangent, jnp.zeros_like(cotangent))
    gathered = lax.all_to_all(tokens, ("y", "z"), split_axis=2, concat_axis=1, tiled=True)
    grad_whole = lax.all_to_all(grad_live, ("y", "z"), split_axis=2, concat_axis=1, tiled=True)
    frame_count = gathered.shape[1]
    patch_count = gathered.shape[2]
    row_count = clip_count * frame_count * patch_count
    grad_scale = 1.0 / math.sqrt(clip_count * rep_size * frame_count * patch_count * seq_size)
    factor = HEAD_DIM ** (-0.5)
    head_shape = (clip_count, frame_count, patch_count, HEADS, HEAD_DIM)
    allowed = jax.vmap(partial(frame_mask, frame_count=frame_count))(windows, window_counts)[
        :, None, None
    ]
    flat_input = gathered.reshape(row_count, D).astype(jnp.float32)
    centred = flat_input - jnp.mean(flat_input, axis=1, keepdims=True)
    inv_std = lax.rsqrt(jnp.mean(centred * centred, axis=1, keepdims=True) + EPSILON)
    normal_hat = centred * inv_std
    normed = (normal_hat * norm_gain + norm_bias).astype(jnp.bfloat16)
    normed_rows = normed.reshape(clip_count, frame_count, patch_count, D)
    grad_rows_in = grad_whole.reshape(clip_count, frame_count, patch_count, D)
    projected = jnp.einsum(
        "cfpk,kn->cpnf", normed_rows, qkv_weight, preferred_element_type=jnp.float32
    ).astype(jnp.bfloat16)
    head_shape = (clip_count, patch_count, 3, HEADS, HEAD_DIM, frame_count)
    projected = projected.reshape(head_shape)
    query_heads = projected[:, :, 0]
    key_heads = projected[:, :, 1]
    value_heads = projected[:, :, 2]
    scores = (
        jnp.einsum("cphdf,cphdg->cphfg", query_heads, key_heads, preferred_element_type=jnp.float32)
        * factor
    )
    row_max = jnp.max(jnp.where(allowed, scores, -1e30), axis=-1, keepdims=True)
    exp_scores = jnp.where(allowed, jnp.exp(scores - row_max), 0.0)
    attn_prob = exp_scores / jnp.sum(exp_scores, axis=-1, keepdims=True)
    prob_bf = attn_prob.astype(jnp.bfloat16)
    attended = jnp.einsum(
        "cphfg,cphdg->cphdf", prob_bf, value_heads, preferred_element_type=jnp.float32
    ).astype(jnp.bfloat16)
    grad_attn = (
        jnp.einsum("cfpn,kn->cpkf", grad_rows_in, out_weight, preferred_element_type=jnp.float32)
        .astype(jnp.bfloat16)
        .reshape(clip_count, patch_count, HEADS, HEAD_DIM, frame_count)
    )
    grad_prob = jnp.einsum(
        "cphdf,cphdg->cphfg", grad_attn, value_heads, preferred_element_type=jnp.float32
    )
    grad_scores = (
        attn_prob * (grad_prob - jnp.sum(attn_prob * grad_prob, axis=-1, keepdims=True)) * factor
    ).astype(jnp.bfloat16)
    grad_scores = lax.optimization_barrier(grad_scores)
    grad_query = jnp.einsum(
        "cphfg,cphdg->cphdf", grad_scores, key_heads, preferred_element_type=jnp.float32
    ).astype(jnp.bfloat16)
    grad_keys = jnp.einsum(
        "cphfg,cphdf->cphdg", grad_scores, query_heads, preferred_element_type=jnp.float32
    ).astype(jnp.bfloat16)
    grad_values = jnp.einsum(
        "cphfg,cphdf->cphdg", prob_bf, grad_attn, preferred_element_type=jnp.float32
    ).astype(jnp.bfloat16)
    grad_cols = jnp.stack([grad_query, grad_keys, grad_values], axis=2).reshape(
        clip_count, patch_count, 3 * D, frame_count
    )
    grad_normed = jnp.einsum(
        "cpnf,kn->cfpk", grad_cols, qkv_weight, preferred_element_type=jnp.float32
    ).reshape(row_count, D)
    gain_term = jnp.sum(grad_normed * normal_hat, axis=0) * grad_scale
    bias_term = jnp.sum(grad_normed, axis=0) * grad_scale
    grad_hat = grad_normed * norm_gain
    grad_norm_in = (
        inv_std
        * (
            grad_hat
            - jnp.mean(grad_hat, axis=1, keepdims=True)
            - normal_hat * jnp.mean(grad_hat * normal_hat, axis=1, keepdims=True)
        )
    ).astype(jnp.bfloat16)
    returned = lax.all_to_all(
        grad_norm_in.reshape(clip_count, frame_count, patch_count, D),
        ("y", "z"),
        split_axis=1,
        concat_axis=2,
        tiled=True,
    )
    grad_input = (grad_live.astype(jnp.float32) + returned.astype(jnp.float32)).astype(jnp.bfloat16)
    side_terms = jnp.stack([gain_term, bias_term]).reshape(2, seq_size, D // seq_size)
    side_terms = lax.all_to_all(side_terms, ("y", "z"), split_axis=1, concat_axis=1, tiled=True)
    side_terms = lax.psum(jnp.sum(side_terms, axis=1), ("x", "core"))
    x_size = lax.axis_size("x")
    width = (3 * D + D) // (2 * x_size)
    core = lax.axis_index("core")

    attended_cols = attended.reshape(clip_count, patch_count, D, frame_count)

    def half_of(index):
        grad_part = lax.dynamic_index_in_dim(
            grad_cols.reshape(clip_count, patch_count, 3 * D // (2 * width), 2, width, frame_count),
            index,
            axis=3,
            keepdims=False,
        ).reshape(clip_count, patch_count, 3 * D // 2, frame_count)
        flat_part = lax.dynamic_slice_in_dim(grad_rows_in, index * width, width, axis=3)
        upper = jnp.einsum(
            "cfpk,cpnf->kn", normed_rows, grad_part, preferred_element_type=jnp.float32
        )
        lower = jnp.einsum(
            "cpnf,cfpm->nm", attended_cols, flat_part, preferred_element_type=jnp.float32
        )
        return (jnp.concatenate([upper, lower], axis=1) * grad_scale).astype(jnp.bfloat16)

    mine = half_of(core)
    got = lax.ppermute(half_of(1 - core), "core", [(0, 1), (1, 0)])
    merged = (mine.astype(jnp.float32) + got.astype(jnp.float32)).astype(jnp.bfloat16)
    merged = lax.psum_scatter(merged.reshape(D, x_size, width), "y", scatter_dimension=0, tiled=True)
    merged = lax.psum_scatter(merged, "z", scatter_dimension=0, tiled=True)
    merged = lax.psum_scatter(merged, "x", scatter_dimension=1, tiled=True)
    summed = lax.all_gather(
        merged.reshape(merged.shape[0], width), ("x", "core"), axis=1, tiled=True
    ).astype(jnp.float32)
    return (grad_input, summed[:, : 3 * D], summed[:, 3 * D :], side_terms[0], side_terms[1])


def fine_mesh(mesh):
    devices = np.asarray(mesh.devices)
    rep_size, seq_size = devices.shape
    y_size = len({device.coords[1] for device in devices.flat})
    return Mesh(
        devices.reshape(rep_size // 2, 2, y_size, seq_size // y_size), ("x", "core", "y", "z")
    )


def solution(mesh):
    rep, seq = ("x", "core"), ("y", "z")
    fine = fine_mesh(mesh)
    return jax.shard_map(
        local,
        mesh=fine,
        in_specs=(
            P(rep, seq, None, None),
            P(rep, seq, None, None),
            P(rep),
            P(rep, None, None),
            P(rep, None),
            P(),
            P(),
            P(),
            P(),
        ),
        out_specs=(P(rep, seq, None, None), P(seq, None), P(seq, None), P(seq), P(seq)),
        check_vma=False,
    )
```

profile of v0, /device:TPU:1, one launch (start us, length us, event | category | flops | bytes accessed | tf_op | source)
XLA Modules:
  0.0 285.1 jit_solution(6854672067384150137)
XLA Ops:
  7.2 2.9 %copy.119 = bf16[2,8,32,1024]{3,1,0,2:T(8,128)(2,1)} copy(bf16[2,8,32,1024]{3,2,1,0:T(8,128)(2,1)} %param.9) | data formatting | bytes 2097152 | tf_op args[0]
  10.1 12.0 %all-to-all-start = ((bf16[2,8,32,1024]{3,1,0,2:T(8,128)(2,1)}), bf16[2,8,32,1024]{3,1,0,2:T(8,128)(2,1)S(1)}, u32[]{:S(2)}, u32[]{:S(2)}) async-start(bf16[2,8,32,1024]{3,1,0,2:T(8,128)(2,1)} %copy.119), calls=%async_computation | async-start | bytes 2097152 | tf_op jit(solution)/shard_map/all_to_all | solution.py:47
  26.8 20.3 %all-to-all-done = bf16[2,8,32,1024]{3,1,0,2:T(8,128)(2,1)S(1)} async-done(((bf16[2,8,32,1024]{3,1,0,2:T(8,128)(2,1)}), bf16[2,8,32,1024]{3,1,0,2:T(8,128)(2,1)S(1)}, u32[]{:S(2)}, u32[]{:S(2)}) %all-to-all-start) | async-done | bytes 1048608 | tf_op jit(solution)/shard_map/all_to_all | solution.py:47
  47.0 8.5 %all-to-all-start.1 = ((bf16[2,8,32,1024]{3,1,0,2:T(8,128)(2,1)}), bf16[2,8,32,1024]{3,1,0,2:T(8,128)(2,1)}, u32[]{:S(2)}, u32[]{:S(2)}) async-start(bf16[2,8,32,1024]{3,1,0,2:T(8,128)(2,1)} %copy.127), calls=%async_computation.1 | async-start | bytes 2097152 | tf_op jit(solution)/shard_map/all_to_all | solution.py:48
  56.6 7.8 %fusion.25 = bf16[2,1,3072,256]{2,3,0,1:T(8,128)(2,1)} fusion(bf16[1024,3072]{1,0:T(8,128)(2,1)} %param.16, f32[1024]{0:T(1024)S(1)} %copy-done.13, f32[1024]{0:T(1024)S(1)} %copy-done.10, f32[2,256]{1,0:T(2,128)S(1)} %rsqrt.13, f32[2,256]{1,0:T(2,128)S(1)} %div.35, bf16[2,8,32,1024]{3,1,0,2:T(8,128)(2,1)S(1)} %all-to-all-done), kind=kOutput, calls=%fused_computation.30 | convolution fusion | flops 3225944064 | bytes 10498048 | tf_op jit(solution)/shard_map/cfpk,kn->cpnf/dot_general | solution.py:65
  64.4 4.6 %copy.121 = bf16[2,1,3072,256]{3,2,0,1:T(8,128)(2,1)} copy(bf16[2,1,3072,256]{2,3,0,1:T(8,128)(2,1)} %fusion.25) | data formatting | bytes 6291456 | tf_op jit(solution)/shard_map/convert_element_type | solution.py:67
  69.0 6.1 %fusion.91 = f32[2,16,256,256]{2,3,1,0:T(8,128)} fusion(bf16[2,1,3,16,64,256]{5,4,3,2,0,1:T(8,128)(2,1)} %bitcast.224), kind=kOutput, calls=%fused_computation.92 | convolution fusion | flops 268435456 | bytes 10485760 | tf_op jit(solution)/shard_map/cphdf,cphdg->cphfg/dot_general | solution.py:74
  75.1 5.6 %all-to-all-done.1 = bf16[2,8,32,1024]{3,1,0,2:T(8,128)(2,1)} async-done(((bf16[2,8,32,1024]{3,1,0,2:T(8,128)(2,1)}), bf16[2,8,32,1024]{3,1,0,2:T(8,128)(2,1)}, u32[]{:S(2)}, u32[]{:S(2)}) %all-to-all-start.1) | async-done | bytes 1048608 | tf_op jit(solution)/shard_map/all_to_all | solution.py:48
  80.7 3.5 %fusion.77 = bf16[2,1,1024,256]{2,3,0,1:T(8,128)(2,1)} fusion(bf16[1024,1024]{1,0:T(8,128)(2,1)S(1)} %copy-done, bf16[2,8,32,1024]{3,1,0,2:T(8,128)(2,1)} %all-to-all-done.1), kind=kOutput, calls=%fused_computation.77 | convolution fusion | flops 1074266112 | bytes 4194304 | tf_op jit(solution)/shard_map/cfpn,kn->cpkf/dot_general | solution.py:85
  85.6 6.1 %fusion.92 = f32[2,16,256,256]{2,3,1,0:T(8,128)} fusion(bf16[2,16,64,256]{3,2,1,0:T(8,128)(2,1)S(1)} %bitcast.235, bf16[2,1,3,16,64,256]{5,4,3,2,0,1:T(8,128)(2,1)} %bitcast.225), kind=kOutput, calls=%fused_computation.93 | convolution fusion | flops 268435456 | bytes 10485760 | tf_op jit(solution)/shard_map/cphdf,cphdg->cphfg/dot_general | solution.py:89
  91.8 5.4 %fusion.114 = (f32[2,16,256]{2,1,0:T(8,128)S(1)}, f32[2,16,256,256]{2,3,1,0:T(8,128)}) fusion(f32[2,16,256,256]{2,3,1,0:T(8,128)S(1)} %copy-done.3, pred[2,256,256]{1,2,0:T(8,128)(4,1)S(1)} %copy.125), kind=kOutput, calls=%fused_computation.131 | output fusion | flops 12583167 | bytes 16941056 | tf_op jit(solution)/shard_map/sub | solution.py:78
  97.2 12.3 %fusion.32 = bf16[2,1,16,256,256]{3,4,2,0,1:T(8,128)(2,1)S(1)} fusion(f32[2,16,256,256]{2,3,1,0:T(8,128)} %fusion.92, f32[2,16,256,256]{2,3,1,0:T(8,128)} %get-tuple-element.33, f32[2,16,256]{2,1,0:T(8,128)S(1)} %get-tuple-element.32), kind=kOutput, calls=%fused_computation.40 | output fusion | flops 14688511 | bytes 21004288 | tf_op jit(solution)/shard_map/sub | solution.py:93
  122.0 2.5 fusion.3
  124.4 4.6 %collective-permute-start = (bf16[1024,2048]{1,0:T(8,128)(2,1)}, bf16[1024,2048]{1,0:T(8,128)(2,1)}, u32[]{:S(2)}, u32[]{:S(2)}) collective-permute-start(bf16[1024,2048]{1,0:T(8,128)(2,1)} %fusion.3), channel_id=1, source_target_pairs={{0,32},{32,0},{1,33},{33,1},{2,34},{34,2},{3,35},{35,3},{4,36},{36... | collective-permute-start | bytes 12582920 | tf_op jit(solution)/shard_map/ppermute | solution.py:156
  133.8 2.3 collective-permute-done
  136.1 3.2 %add_convert_fusion = bf16[1024,2048]{1,0:T(8,128)(2,1)S(1)} fusion(bf16[1024,2048]{1,0:T(8,128)(2,1)} %collective-permute-done, f32[1024,512]{1,0:T(8,128)S(1)} %convolution_bitcast_fusion.3, f32[1024,1536]{1,0:T(8,128)S(1)} %convolution_bitcast_fusion.1), kind=kLoop, calls=%fused_computation.6 | loop fusion | flops 14680064 | bytes 16777216 | tf_op jit(solution)/shard_map/convert_element_type | solution.py:157
  143.4 6.4 %fusion.53 = (f32[1024]{0:T(1024)S(1)}, f32[2,256]{1,0:T(2,128)S(1)}, f32[2,256]{1,0:T(2,128)S(1)}, f32[2,256,1024]{2,1,0:T(8,128)S(1)}) fusion(f32[2,256]{1,0:T(2,128)S(1)} %div.35, f32[2,256]{1,0:T(2,128)S(1)} %rsqrt.13, bf16[2,8,32,1024]{3,1,0,2:T(8,128)(2,1)S(1)} %all-to-all-done, f32[1024]{0:T(1024)S(1)} %copy-done.10, ...), kind=kOutput, calls=%fused_computation.59 | convolution fusion | flops 3225942016 | bytes 12599296 | tf_op jit(solution)/shard_map/cpnf,kn->cfpk/dot_general | solution.py:108
  150.7 4.7 %all-to-all-start.3 = ((f32[2,32,32]{2,0,1:T(2,128)}), f32[2,32,32]{2,0,1:T(2,128)S(1)}, u32[]{:S(2)}, u32[]{:S(2)}) async-start(f32[2,32,32]{2,0,1:T(2,128)} %pad_maximum_fusion.2), calls=%async_computation.6 | async-start | bytes 65536 | tf_op jit(solution)/shard_map/all_to_all | solution.py:131
  155.5 32.1 %reduce-scatter.4.cloned.1.call-done = bf16[256,4,512]{2,0,1:T(8,128)(2,1)} async-done(((bf16[1024,4,512]{2,0,1:T(8,128)(2,1)}), bf16[256,4,512]{2,0,1:T(8,128)(2,1)}) %reduce-scatter.4.cloned.1.call-update) | async-done | bytes 1048592 | tf_op jit(solution)/shard_map/reduce_scatter | solution.py:158
  190.3 8.2 %all-to-all-start.2 = ((bf16[2,256,1,1024]{3,0,2,1:T(2,128)(2,1)}), bf16[2,256,1,1024]{3,0,2,1:T(2,128)(2,1)}, u32[]{:S(2)}, u32[]{:S(2)}) async-start(bf16[2,256,1,1024]{3,0,2,1:T(2,128)(2,1)} %copy.136), calls=%async_computation.2 | async-start | bytes 2097152 | tf_op jit(solution)/shard_map/all_to_all | solution.py:122
  198.6 13.2 %psum.7 = f32[2,32]{1,0:T(2,128)S(1)} all-reduce(f32[2,32]{1,0:T(2,128)S(1)} %reduce_sum.89), channel_id=1, replica_groups=mesh['x'=4,'core'=2,'y'=4,'z'=8] {'x','core'}, use_global_device_ids=true, to_apply=%region_14.15 | all-reduce | flops 64 | bytes 512 | tf_op jit(solution)/shard_map/psum | solution.py:132
  212.3 23.6 %reduce-scatter.6.cloned.1.call-done = bf16[32,4,512]{2,0,1:T(8,128)(2,1)} async-done(((bf16[256,4,512]{2,0,1:T(8,128)(2,1)}), bf16[32,4,512]{2,0,1:T(8,128)(2,1)}) %reduce-scatter.6.cloned.1.call-update) | async-done | bytes 131088 | tf_op jit(solution)/shard_map/reduce_scatter | solution.py:159
  239.7 21.6 %reduce-scatter.8.cloned.1.call-done = bf16[32,1,512]{2,0,1:T(8,128)(2,1)} async-done(((bf16[32,4,512]{2,0,1:T(8,128)(2,1)}), bf16[32,1,512]{2,0,1:T(8,128)(2,1)}) %reduce-scatter.8.cloned.1.call-update) | async-done | bytes 32784 | tf_op jit(solution)/shard_map/reduce_scatter | solution.py:160
  261.2 15.8 %all-gather = bf16[32,1,4096]{2,0,1:T(8,128)(2,1)S(1)} all-gather(bf16[32,1,512]{2,0,1:T(8,128)(2,1)} %reduce-scatter.8.cloned.1.call-done), channel_id=2, replica_groups=mesh['x'=4,'core'=2,'y'=4,'z'=8] {'x','core'}, dimensions={2}, use_global_device_ids=true | all-gather | bytes 294912 | tf_op jit(solution)/shard_map/all_gather | solution.py:161
  (90 shorter events, 37.3 us)
Async XLA Ops:
  7.2 73.5 %copy-start = (bf16[1024,1024]{1,0:T(8,128)(2,1)S(1)}, bf16[1024,1024]{1,0:T(8,128)(2,1)}, u32[]{:S(2)}) copy-start(bf16[1024,1024]{1,0:T(8,128)(2,1)} %param.17) | copy-start | bytes 6291460
  7.2 15.0 %copy-start.11 = (s32[2,4,3]{1,0,2:T(2,128)S(1)}, s32[2,4,3]{1,0,2:T(2,128)}, u32[]{:S(2)}) copy-start(s32[2,4,3]{1,0,2:T(2,128)} %param.12) | copy-start | bytes 292
  7.2 15.0 %copy-start.12 = (s32[2,4]{1,0:T(2,128)S(1)}, s32[2,4]{1,0:T(2,128)}, u32[]{:S(2)}) copy-start(s32[2,4]{1,0:T(2,128)} %param.13) | copy-start | bytes 100
  10.1 36.9 %all-to-all-start = ((bf16[2,8,32,1024]{3,1,0,2:T(8,128)(2,1)}), bf16[2,8,32,1024]{3,1,0,2:T(8,128)(2,1)S(1)}, u32[]{:S(2)}, u32[]{:S(2)}) async-start(bf16[2,8,32,1024]{3,1,0,2:T(8,128)(2,1)} %copy.119), calls=%async_computation | async-start | bytes 2097152 | tf_op jit(solution)/shard_map/all_to_all | solution.py:47
  25.6 31.0 %copy-start.10 = (f32[1024]{0:T(1024)S(1)}, f32[1024]{0:T(1024)}, u32[]{:S(2)}) copy-start(f32[1024]{0:T(1024)} %param.14) | copy-start | bytes 12292
  25.6 31.0 %copy-start.13 = (f32[1024]{0:T(1024)S(1)}, f32[1024]{0:T(1024)}, u32[]{:S(2)}) copy-start(f32[1024]{0:T(1024)} %param.15) | copy-start | bytes 12292
  47.0 33.6 %all-to-all-start.1 = ((bf16[2,8,32,1024]{3,1,0,2:T(8,128)(2,1)}), bf16[2,8,32,1024]{3,1,0,2:T(8,128)(2,1)}, u32[]{:S(2)}, u32[]{:S(2)}) async-start(bf16[2,8,32,1024]{3,1,0,2:T(8,128)(2,1)} %copy.127), calls=%async_computation.1 | async-start | bytes 2097152 | tf_op jit(solution)/shard_map/all_to_all | solution.py:48
  55.5 132.0 %reduce-scatter.4.cloned.1.call-start = ((), (), s32[]{:S(2)}) async-start(), calls=%async_computation.7 | async-start | bytes 5242880 | tf_op jit(solution)/shard_map/reduce_scatter | solution.py:158
  85.6 6.2 %copy-start.4 = (bf16[2,1,1024,256]{3,2,0,1:T(8,128)(2,1)}, bf16[2,1,1024,256]{3,2,0,1:T(8,128)(2,1)S(1)}, u32[]{:S(2)}) copy-start(bf16[2,1,1024,256]{3,2,0,1:T(8,128)(2,1)S(1)} %copy.129) | copy-start | bytes 3145732
  85.6 6.2 %copy-start.3 = (f32[2,16,256,256]{2,3,1,0:T(8,128)S(1)}, f32[2,16,256,256]{2,3,1,0:T(8,128)}, u32[]{:S(2)}) copy-start(f32[2,16,256,256]{2,3,1,0:T(8,128)} %fusion.91) | copy-start | bytes 25165828
  97.2 12.3 %copy-start.2 = (bf16[2,1,3072,256]{3,2,0,1:T(8,128)(2,1)S(1)}, bf16[2,1,3072,256]{3,2,0,1:T(8,128)(2,1)}, u32[]{:S(2)}) copy-start(bf16[2,1,3072,256]{3,2,0,1:T(8,128)(2,1)} %copy.121) | copy-start | bytes 9437188
  109.5 3.4 %copy-start.16 = (f32[2,16,256,256]{2,3,1,0:T(8,128)S(1)}, f32[2,16,256,256]{2,3,1,0:T(8,128)}, u32[]{:S(2)}) copy-start(f32[2,16,256,256]{2,3,1,0:T(8,128)} %get-tuple-element.33) | copy-start | bytes 25165828
  110.3 3.0 %copy-start.5 = (bf16[2,1,1024,256]{3,2,0,1:T(8,128)(2,1)S(1)}, bf16[2,1,1024,256]{3,2,0,1:T(8,128)(2,1)}, u32[]{:S(2)}) copy-start(bf16[2,1,1024,256]{3,2,0,1:T(8,128)(2,1)} %copy-done.4) | copy-start | bytes 3145732
  115.6 3.3 %copy-start.14 = (bf16[2,16,64,256]{3,2,1,0:T(8,128)(2,1)}, bf16[2,16,64,256]{3,2,1,0:T(8,128)(2,1)S(1)}, u32[]{:S(2)}) copy-start(bf16[2,16,64,256]{3,2,1,0:T(8,128)(2,1)S(1)} %fusion.65) | copy-start | bytes 3145732
  118.9 1.0 copy-start.8
  124.4 11.7 %collective-permute-start = (bf16[1024,2048]{1,0:T(8,128)(2,1)}, bf16[1024,2048]{1,0:T(8,128)(2,1)}, u32[]{:S(2)}, u32[]{:S(2)}) collective-permute-start(bf16[1024,2048]{1,0:T(8,128)(2,1)} %fusion.3), channel_id=1, source_target_pairs={{0,32},{32,0},{1,33},{33,1},{2,34},{34,2},{3,35},{35,3},{4,36},{36... | collective-permute-start | bytes 12582920 | tf_op jit(solution)/shard_map/ppermute | solution.py:156
  129.0 1.7 copy-start.9
  129.0 2.0 copy-start.15
  150.7 39.6 %all-to-all-start.3 = ((f32[2,32,32]{2,0,1:T(2,128)}), f32[2,32,32]{2,0,1:T(2,128)S(1)}, u32[]{:S(2)}, u32[]{:S(2)}) async-start(f32[2,32,32]{2,0,1:T(2,128)} %pad_maximum_fusion.2), calls=%async_computation.6 | async-start | bytes 65536 | tf_op jit(solution)/shard_map/all_to_all | solution.py:131
  155.4 80.5 %reduce-scatter.6.cloned.1.call-start = ((), (), s32[]{:S(2)}) async-start(), calls=%async_computation.8 | async-start | bytes 1179648 | tf_op jit(solution)/shard_map/reduce_scatter | solution.py:159
  188.2 47.7 %copy-start.6 = (bf16[2,8,32,1024]{3,2,1,0:T(8,128)(2,1)S(1)}, bf16[2,8,32,1024]{3,2,1,0:T(8,128)(2,1)}, u32[]{:S(2)}) copy-start(bf16[2,8,32,1024]{3,2,1,0:T(8,128)(2,1)} %param.10) | copy-start | bytes 3145732
  190.3 45.6 %all-to-all-start.2 = ((bf16[2,256,1,1024]{3,0,2,1:T(2,128)(2,1)}), bf16[2,256,1,1024]{3,0,2,1:T(2,128)(2,1)}, u32[]{:S(2)}, u32[]{:S(2)}) async-start(bf16[2,256,1,1024]{3,0,2,1:T(2,128)(2,1)} %copy.136), calls=%async_computation.2 | async-start | bytes 2097152 | tf_op jit(solution)/shard_map/all_to_all | solution.py:122
  198.5 62.7 %reduce-scatter.8.cloned.1.call-start = ((), (), s32[]{:S(2)}) async-start(), calls=%async_computation.9 | async-start | bytes 163840 | tf_op jit(solution)/shard_map/reduce_scatter | solution.py:160
  235.9 42.6 %copy-start.1 = (bf16[1024,1024]{1,0:T(8,128)(2,1)S(1)}, bf16[1024,1024]{1,0:T(8,128)(2,1)}, u32[]{:S(2)}) copy-start(bf16[1024,1024]{1,0:T(8,128)(2,1)} %param.17) | copy-start | bytes 6291460
  (1 other events, 1.0 us)
Sparse Core Ops, SparseCore 0:
  141.7 45.8 reduce-scatter.3
  190.1 45.7 reduce-scatter.5
  238.4 22.7 reduce-scatter.7
where the time goes:
time: 286 us; the launch traced here: 285 us
  waiting for transfers between devices  105 us (37%)
  matrix products  40.6 us (14%)
  starting transfers between devices  38.2 us (13%)
  other arithmetic  31.5 us (11%)
  blocking collectives  29 us (10%)
  local copies, waits for them, and re-layouts  25.6 us (9%)
  between operations  14.8 us (5%)
    reduce_scatter x1, waiting for transfers between devices, local(): lax.psum_scatter(merged.reshape(D, x_size, width), 'y', scatter_dimension...  32.1 us
    reduce_scatter x1, waiting for transfers between devices, local(): merged = lax.psum_scatter(merged, 'z', scatter_dimension=0, tiled=True)  23.6 us
    reduce_scatter x1, waiting for transfers between devices, local(): merged = lax.psum_scatter(merged, 'x', scatter_dimension=1, tiled=True)  21.6 us
    all_to_all x1, waiting for transfers between devices, local(): lax.all_to_all(tokens, ('y', 'z'), split_axis=2, concat_axis=1, tiled=True)  20.3 us
    all_gather x1, blocking collectives, local(): lax.all_gather(merged.reshape(merged.shape[0], width), ('x', 'core'), axi...  15.8 us
    psum x1, blocking collectives, local(): side_terms = lax.psum(jnp.sum(side_terms, axis=1), ('x', 'core'))  13.2 us
    sub x1, other arithmetic, local(): grad_prob - jnp.sum(attn_prob * grad_prob, axis=-1, keepdims=True)  12.3 us
    all_to_all x1, starting transfers between devices, local(): lax.all_to_all(tokens, ('y', 'z'), split_axis=2, concat_axis=1, tiled=True)  12 us
  transfers between devices with their start and end apart: 8, of which 6 were waited for; matrix products, arithmetic and copies ran while one was open for 15% of the time, Pallas kernels for 0%

commit v1 on v0

--- a/solution.py
+++ b/solution.py
@@ -92,12 +92,14 @@
     grad_scores = (
         attn_prob * (grad_prob - jnp.sum(attn_prob * grad_prob, axis=-1, keepdims=True)) * factor
     ).astype(jnp.bfloat16)
-    grad_scores = lax.optimization_barrier(grad_scores)
+    grad_scores, grad_scores_t = lax.optimization_barrier(
+        (grad_scores, jnp.swapaxes(grad_scores, -1, -2))
+    )
     grad_query = jnp.einsum(
         "cphfg,cphdg->cphdf", grad_scores, key_heads, preferred_element_type=jnp.float32
     ).astype(jnp.bfloat16)
     grad_keys = jnp.einsum(
-        "cphfg,cphdf->cphdg", grad_scores, query_heads, preferred_element_type=jnp.float32
+        "cphgf,cphdf->cphdg", grad_scores_t, query_heads, preferred_element_type=jnp.float32
     ).astype(jnp.bfloat16)
     grad_values = jnp.einsum(
         "cphfg,cphdf->cphdg", prob_bf, grad_attn, preferred_element_type=jnp.float32

time: 286 us -> 297 us (1.038)
  waiting for transfers between devices: 105 us -> 123 us
  other arithmetic: 31.5 us -> 19.3 us
  matrix products: 40.6 us -> 48.4 us
    all_to_all x1, waiting for transfers between devices: 5.56 us -> 23.1 us  [local(): lax.all_to_all(grad_live, ('y', 'z'), split_axis=2, concat_axis=1, tiled=...]
    sub x1 -> x0, other arithmetic: 12.3 us -> none  [local(): grad_prob - jnp.sum(attn_prob * grad_prob, axis=-1, keepdims=True)]
    sub x0 -> x1, matrix products: none -> 10.7 us  [local(): grad_prob - jnp.sum(attn_prob * grad_prob, axis=-1, keepdims=True)]
    dot_general x2 -> x1, matrix products: 7.52 us -> 1.39 us  [local(): jnp.einsum('cphgf,cphdf->cphdg', grad_scores_t, query_heads, preferred_el...]
    dot_general x1, matrix products: 6.06 us -> 1.3 us  [local(): jnp.einsum('cphdf,cphdg->cphfg', query_heads, key_heads, preferred_elemen...]
    dot_general x1, matrix products: 1.4 us -> 5.87 us  [local(): jnp.einsum('cphfg,cphdf->cphdg', prob_bf, grad_attn, preferred_element_ty...]
    dot_general x1, matrix products: 0.94 us -> 4.38 us  [local(): jnp.einsum('cphfg,cphdg->cphdf', prob_bf, value_heads, preferred_element_...]
    unnamed x37 -> x43, local copies, waits for them, and re-layouts: 6.71 us -> 8.61 us
  transfers between devices with their start and end apart: 8 -> 8, of which waited for: 6 -> 6; matrix products, arithmetic and copies ran while one was open for 15% -> 8% of each run, Pallas kernels for 0% -> 0%
where the time goes in v1:
time: 297 us
  waiting for transfers between devices  123 us (41%)
  matrix products  48.4 us (16%)
  starting transfers between devices  38.2 us (13%)
  blocking collectives  29 us (10%)
  local copies, waits for them, and re-layouts  24.1 us (8%)
  other arithmetic  19.3 us (6%)
  between operations  14.8 us (5%)
    reduce_scatter x1, waiting for transfers between devices, local(): lax.psum_scatter(merged.reshape(D, x_size, width), 'y', scatter_dimension...  30.5 us
    reduce_scatter x1, waiting for transfers between devices, local(): merged = lax.psum_scatter(merged, 'z', scatter_dimension=0, tiled=True)  23.9 us
    all_to_all x1, waiting for transfers between devices, local(): lax.all_to_all(grad_live, ('y', 'z'), split_axis=2, concat_axis=1, tiled=...  23.1 us
    all_to_all x1, waiting for transfers between devices, local(): lax.all_to_all(tokens, ('y', 'z'), split_axis=2, concat_axis=1, tiled=True)  21.3 us
    reduce_scatter x1, waiting for transfers between devices, local(): merged = lax.psum_scatter(merged, 'x', scatter_dimension=1, tiled=True)  21.2 us
    all_gather x1, blocking collectives, local(): lax.all_gather(merged.reshape(merged.shape[0], width), ('x', 'core'), axi...  15.8 us
    psum x1, blocking collectives, local(): side_terms = lax.psum(jnp.sum(side_terms, axis=1), ('x', 'core'))  13.2 us
    all_to_all x1, starting transfers between devices, local(): lax.all_to_all(tokens, ('y', 'z'), split_axis=2, concat_axis=1, tiled=True)  12 us
  transfers between devices with their start and end apart: 8, of which 6 were waited for; matrix products, arithmetic and copies ran while one was open for 8% of the time, Pallas kernels for 0%

profile of v1, /device:TPU:1, one launch (start us, length us, event | category | flops | bytes accessed | tf_op | source)
XLA Modules:
  0.0 296.5 jit_solution(12532710383796686654)
XLA Ops:
  7.2 2.9 copy.115
  10.1 12.0 %all-to-all-start = ((bf16[2,8,32,1024]{3,1,0,2:T(8,128)(2,1)}), bf16[2,8,32,1024]{3,1,0,2:T(8,128)(2,1)S(1)}, u32[]{:S(2)}, u32[]{:S(2)}) async-start(bf16[2,8,32,1024]{3,1,0,2:T(8,128)(2,1)} %copy.115), calls=%async_computation | async-start | bytes 2097152 | tf_op jit(solution)/shard_map/all_to_all | solution.py:47
  25.8 21.3 %all-to-all-done = bf16[2,8,32,1024]{3,1,0,2:T(8,128)(2,1)S(1)} async-done(((bf16[2,8,32,1024]{3,1,0,2:T(8,128)(2,1)}), bf16[2,8,32,1024]{3,1,0,2:T(8,128)(2,1)S(1)}, u32[]{:S(2)}, u32[]{:S(2)}) %all-to-all-start) | async-done | bytes 1048608 | tf_op jit(solution)/shard_map/all_to_all | solution.py:47
  47.0 8.5 %all-to-all-start.1 = ((bf16[2,8,32,1024]{3,1,0,2:T(8,128)(2,1)}), bf16[2,8,32,1024]{3,1,0,2:T(8,128)(2,1)}, u32[]{:S(2)}, u32[]{:S(2)}) async-start(bf16[2,8,32,1024]{3,1,0,2:T(8,128)(2,1)} %copy.123), calls=%async_computation.1 | async-start | bytes 2097152 | tf_op jit(solution)/shard_map/all_to_all | solution.py:48
  57.5 23.1 %all-to-all-done.1 = bf16[2,8,32,1024]{3,1,0,2:T(8,128)(2,1)} async-done(((bf16[2,8,32,1024]{3,1,0,2:T(8,128)(2,1)}), bf16[2,8,32,1024]{3,1,0,2:T(8,128)(2,1)}, u32[]{:S(2)}, u32[]{:S(2)}) %all-to-all-start.1) | async-done | bytes 1048608 | tf_op jit(solution)/shard_map/all_to_all | solution.py:48
  80.6 3.5 %fusion.74 = bf16[2,1,1024,256]{2,3,0,1:T(8,128)(2,1)} fusion(bf16[1024,1024]{1,0:T(8,128)(2,1)S(1)} %copy-done, bf16[2,8,32,1024]{3,1,0,2:T(8,128)(2,1)} %all-to-all-done.1), kind=kOutput, calls=%fused_computation.76 | convolution fusion | flops 1074266112 | bytes 4194304 | tf_op jit(solution)/shard_map/cfpn,kn->cpkf/dot_general | solution.py:85
  86.4 7.8 %fusion.25 = bf16[2,1,3072,256]{2,3,0,1:T(8,128)(2,1)} fusion(bf16[1024,3072]{1,0:T(8,128)(2,1)} %param.16, f32[1024]{0:T(1024)S(1)} %copy-done.17, f32[1024]{0:T(1024)S(1)} %copy-done.14, f32[2,256]{1,0:T(2,128)S(1)} %rsqrt.13, f32[2,256]{1,0:T(2,128)S(1)} %div.35, bf16[2,8,32,1024]{3,1,0,2:T(8,128)(2,1)S(1)} %all-to-all-done), kind=kOutput, calls=%fused_computation.30 | convolution fusion | flops 3225944064 | bytes 10498048 | tf_op jit(solution)/shard_map/cfpk,kn->cpnf/dot_general | solution.py:65
  94.2 3.2 %copy.117 = bf16[2,1,3072,256]{3,2,0,1:T(8,128)(2,1)S(1)} copy(bf16[2,1,3072,256]{2,3,0,1:T(8,128)(2,1)} %fusion.25) | data formatting | bytes 6291456 | tf_op jit(solution)/shard_map/convert_element_type | solution.py:67
  98.7 5.4 %fusion.113 = (f32[2,16,256]{2,1,0:T(8,128)S(1)}, f32[2,16,256,256]{2,3,1,0:T(8,128)}) fusion(f32[2,16,256,256]{2,3,1,0:T(8,128)S(1)} %fusion.90, pred[2,256,256]{1,2,0:T(8,128)(4,1)S(1)} %copy.121), kind=kOutput, calls=%fused_computation.131 | output fusion | flops 12583167 | bytes 16941056 | tf_op jit(solution)/shard_map/sub | solution.py:78
  104.1 5.9 %fusion.59 = bf16[2,16,64,256]{3,2,1,0:T(8,128)(2,1)} fusion(bf16[2,16,64,256]{3,2,1,0:T(8,128)(2,1)S(1)} %bitcast.253, f32[2,16,256,256]{2,3,1,0:T(8,128)} %get-tuple-element.37, f32[2,16,256]{2,1,0:T(8,128)S(1)} %get-tuple-element.36), kind=kOutput, calls=%fused_computation.71 | convolution fusion | flops 273154048 | bytes 10518528 | tf_op jit(solution)/shard_map/cphfg,cphdf->cphdg/dot_general | solution.py:104
  110.0 10.7 %multiply_convert_fusion = bf16[2,16,256,256]{2,3,1,0:T(8,128)(2,1)} fusion(bf16[2,16,64,256]{3,2,1,0:T(8,128)(2,1)} %bitcast.252, bf16[2,1,3,16,64,256]{5,4,3,2,0,1:T(8,128)(2,1)S(1)} %bitcast.233, f32[2,16,256,256]{2,3,1,0:T(8,128)} %get-tuple-element.37, f32[2,16,256]{2,1,0:T(8,128)S(1)} %get-tuple-element.36), kind=kOutput, calls=%fused_computation.7 | convolution fusion | flops 551559424 | bytes 25231360 | tf_op jit(solution)/shard_map/sub | solution.py:93
  120.7 4.4 %fusion.62 = bf16[2,16,64,256]{3,2,1,0:T(8,128)(2,1)S(1)} fusion(bf16[2,1,3,16,64,256]{5,4,3,2,0,1:T(8,128)(2,1)S(1)} %bitcast.234, f32[2,16,256,256]{2,3,1,0:T(8,128)} %get-tuple-element.37, f32[2,16,256]{2,1,0:T(8,128)S(1)} %get-tuple-element.36), kind=kOutput, calls=%fused_computation.72 | convolution fusion | flops 273154048 | bytes 10518528 | tf_op jit(solution)/shard_map/cphfg,cphdg->cphdf/dot_general | solution.py:81
  133.5 2.5 fusion.3
  136.0 4.6 %collective-permute-start = (bf16[1024,2048]{1,0:T(8,128)(2,1)}, bf16[1024,2048]{1,0:T(8,128)(2,1)}, u32[]{:S(2)}, u32[]{:S(2)}) collective-permute-start(bf16[1024,2048]{1,0:T(8,128)(2,1)} %fusion.3), channel_id=1, source_target_pairs={{0,32},{32,0},{1,33},{33,1},{2,34},{34,2},{3,35},{35,3},{4,36},{36... | collective-permute-start | bytes 12582920 | tf_op jit(solution)/shard_map/ppermute | solution.py:158
  144.9 2.8 collective-permute-done
  147.7 3.2 %add_convert_fusion = bf16[1024,2048]{1,0:T(8,128)(2,1)S(1)} fusion(bf16[1024,2048]{1,0:T(8,128)(2,1)} %collective-permute-done, f32[1024,512]{1,0:T(8,128)S(1)} %convolution_bitcast_fusion.3, f32[1024,1536]{1,0:T(8,128)S(1)} %convolution_bitcast_fusion.1), kind=kLoop, calls=%fused_computation.6 | loop fusion | flops 14680064 | bytes 16777216 | tf_op jit(solution)/shard_map/convert_element_type | solution.py:159
  156.4 6.4 %fusion.50 = (f32[1024]{0:T(1024)S(1)}, f32[2,256]{1,0:T(2,128)S(1)}, f32[2,256]{1,0:T(2,128)S(1)}, f32[2,256,1024]{2,1,0:T(8,128)S(1)}) fusion(f32[2,256]{1,0:T(2,128)S(1)} %div.35, f32[2,256]{1,0:T(2,128)S(1)} %rsqrt.13, bf16[2,8,32,1024]{3,1,0,2:T(8,128)(2,1)S(1)} %copy-done.4, f32[1024]{0:T(1024)S(1)} %copy-done.14, ...), kind=kOutput, calls=%fused_computation.58 | convolution fusion | flops 3225942016 | bytes 12599296 | tf_op jit(solution)/shard_map/cpnf,kn->cfpk/dot_general | solution.py:110
  163.8 4.6 %all-to-all-start.3 = ((f32[2,32,32]{2,0,1:T(2,128)}), f32[2,32,32]{2,0,1:T(2,128)S(1)}, u32[]{:S(2)}, u32[]{:S(2)}) async-start(f32[2,32,32]{2,0,1:T(2,128)} %pad_maximum_fusion.2), calls=%async_computation.6 | async-start | bytes 65536 | tf_op jit(solution)/shard_map/all_to_all | solution.py:133
  168.5 30.5 %reduce-scatter.4.cloned.1.call-done = bf16[256,4,512]{2,0,1:T(8,128)(2,1)} async-done(((bf16[1024,4,512]{2,0,1:T(8,128)(2,1)}), bf16[256,4,512]{2,0,1:T(8,128)(2,1)}) %reduce-scatter.4.cloned.1.call-update) | async-done | bytes 1048592 | tf_op jit(solution)/shard_map/reduce_scatter | solution.py:160
  201.8 8.2 %all-to-all-start.2 = ((bf16[2,256,1,1024]{3,0,2,1:T(2,128)(2,1)}), bf16[2,256,1,1024]{3,0,2,1:T(2,128)(2,1)}, u32[]{:S(2)}, u32[]{:S(2)}) async-start(bf16[2,256,1,1024]{3,0,2,1:T(2,128)(2,1)} %copy.131), calls=%async_computation.2 | async-start | bytes 2097152 | tf_op jit(solution)/shard_map/all_to_all | solution.py:124
  210.1 13.2 %psum.7 = f32[2,32]{1,0:T(2,128)S(1)} all-reduce(f32[2,32]{1,0:T(2,128)S(1)} %reduce_sum.89), channel_id=1, replica_groups=mesh['x'=4,'core'=2,'y'=4,'z'=8] {'x','core'}, use_global_device_ids=true, to_apply=%region_14.15 | all-reduce | flops 64 | bytes 512 | tf_op jit(solution)/shard_map/psum | solution.py:134
  223.8 23.9 %reduce-scatter.6.cloned.1.call-done = bf16[32,4,512]{2,0,1:T(8,128)(2,1)} async-done(((bf16[256,4,512]{2,0,1:T(8,128)(2,1)}), bf16[32,4,512]{2,0,1:T(8,128)(2,1)}) %reduce-scatter.6.cloned.1.call-update) | async-done | bytes 131088 | tf_op jit(solution)/shard_map/reduce_scatter | solution.py:161
  251.5 21.2 %reduce-scatter.8.cloned.1.call-done = bf16[32,1,512]{2,0,1:T(8,128)(2,1)} async-done(((bf16[32,4,512]{2,0,1:T(8,128)(2,1)}), bf16[32,1,512]{2,0,1:T(8,128)(2,1)}) %reduce-scatter.8.cloned.1.call-update) | async-done | bytes 32784 | tf_op jit(solution)/shard_map/reduce_scatter | solution.py:162
  272.7 15.8 %all-gather = bf16[32,1,4096]{2,0,1:T(8,128)(2,1)S(1)} all-gather(bf16[32,1,512]{2,0,1:T(8,128)(2,1)} %reduce-scatter.8.cloned.1.call-done), channel_id=2, replica_groups=mesh['x'=4,'core'=2,'y'=4,'z'=8] {'x','core'}, dimensions={2}, use_global_device_ids=true | all-gather | bytes 294912 | tf_op jit(solution)/shard_map/all_gather | solution.py:163
  (95 shorter events, 36.3 us)
Async XLA Ops:
  7.2 73.5 %copy-start = (bf16[1024,1024]{1,0:T(8,128)(2,1)S(1)}, bf16[1024,1024]{1,0:T(8,128)(2,1)}, u32[]{:S(2)}) copy-start(bf16[1024,1024]{1,0:T(8,128)(2,1)} %param.17) | copy-start | bytes 6291460
  10.1 36.9 %all-to-all-start = ((bf16[2,8,32,1024]{3,1,0,2:T(8,128)(2,1)}), bf16[2,8,32,1024]{3,1,0,2:T(8,128)(2,1)S(1)}, u32[]{:S(2)}, u32[]{:S(2)}) async-start(bf16[2,8,32,1024]{3,1,0,2:T(8,128)(2,1)} %copy.115), calls=%async_computation | async-start | bytes 2097152 | tf_op jit(solution)/shard_map/all_to_all | solution.py:47
  22.8 32.9 %copy-start.15 = (s32[2,4,3]{1,0,2:T(2,128)S(1)}, s32[2,4,3]{1,0,2:T(2,128)}, u32[]{:S(2)}) copy-start(s32[2,4,3]{1,0,2:T(2,128)} %param.12) | copy-start | bytes 292
  22.8 32.9 %copy-start.16 = (s32[2,4]{1,0:T(2,128)S(1)}, s32[2,4]{1,0:T(2,128)}, u32[]{:S(2)}) copy-start(s32[2,4]{1,0:T(2,128)} %param.13) | copy-start | bytes 100
  47.0 39.4 %copy-start.3 = (bf16[2,8,32,1024]{3,1,0,2:T(8,128)(2,1)}, bf16[2,8,32,1024]{3,1,0,2:T(8,128)(2,1)S(1)}, u32[]{:S(2)}) copy-start(bf16[2,8,32,1024]{3,1,0,2:T(8,128)(2,1)S(1)} %all-to-all-done) | copy-start | bytes 3145732
  47.0 33.6 %all-to-all-start.1 = ((bf16[2,8,32,1024]{3,1,0,2:T(8,128)(2,1)}), bf16[2,8,32,1024]{3,1,0,2:T(8,128)(2,1)}, u32[]{:S(2)}, u32[]{:S(2)}) async-start(bf16[2,8,32,1024]{3,1,0,2:T(8,128)(2,1)} %copy.123), calls=%async_computation.1 | async-start | bytes 2097152 | tf_op jit(solution)/shard_map/all_to_all | solution.py:48
  55.5 143.6 %reduce-scatter.4.cloned.1.call-start = ((), (), s32[]{:S(2)}) async-start(), calls=%async_computation.7 | async-start | bytes 5242880 | tf_op jit(solution)/shard_map/reduce_scatter | solution.py:160
  57.5 28.9 %copy-start.14 = (f32[1024]{0:T(1024)S(1)}, f32[1024]{0:T(1024)}, u32[]{:S(2)}) copy-start(f32[1024]{0:T(1024)} %param.14) | copy-start | bytes 12292
  57.5 28.9 %copy-start.17 = (f32[1024]{0:T(1024)S(1)}, f32[1024]{0:T(1024)}, u32[]{:S(2)}) copy-start(f32[1024]{0:T(1024)} %param.15) | copy-start | bytes 12292
  98.7 5.4 %copy-start.13 = (bf16[2,1,1024,256]{3,2,0,1:T(8,128)(2,1)S(1)}, bf16[2,1,1024,256]{3,2,0,1:T(8,128)(2,1)}, u32[]{:S(2)}) copy-start(bf16[2,1,1024,256]{3,2,0,1:T(8,128)(2,1)} %copy.125) | copy-start | bytes 3145732
  120.7 4.6 %copy-start.2 = (bf16[2,16,256,256]{2,3,1,0:T(8,128)(2,1)S(1)}, bf16[2,16,256,256]{2,3,1,0:T(8,128)(2,1)}, u32[]{:S(2)}) copy-start(bf16[2,16,256,256]{2,3,1,0:T(8,128)(2,1)} %multiply_convert_fusion) | copy-start | bytes 12582916
  125.1 5.3 %copy-start.18 = (bf16[2,16,64,256]{3,2,1,0:T(8,128)(2,1)}, bf16[2,16,64,256]{3,2,1,0:T(8,128)(2,1)S(1)}, u32[]{:S(2)}) copy-start(bf16[2,16,64,256]{3,2,1,0:T(8,128)(2,1)S(1)} %fusion.62) | copy-start | bytes 3145732
  126.7 1.6 copy-start.10
  129.0 2.4 copy-start.4
  136.0 11.7 %collective-permute-start = (bf16[1024,2048]{1,0:T(8,128)(2,1)}, bf16[1024,2048]{1,0:T(8,128)(2,1)}, u32[]{:S(2)}, u32[]{:S(2)}) collective-permute-start(bf16[1024,2048]{1,0:T(8,128)(2,1)} %fusion.3), channel_id=1, source_target_pairs={{0,32},{32,0},{1,33},{33,1},{2,34},{34,2},{3,35},{35,3},{4,36},{36... | collective-permute-start | bytes 12582920 | tf_op jit(solution)/shard_map/ppermute | solution.py:158
  140.5 1.2 copy-start.12
  140.5 1.5 copy-start.19
  153.1 1.5 copy-start.8
  163.8 38.0 %all-to-all-start.3 = ((f32[2,32,32]{2,0,1:T(2,128)}), f32[2,32,32]{2,0,1:T(2,128)S(1)}, u32[]{:S(2)}, u32[]{:S(2)}) async-start(f32[2,32,32]{2,0,1:T(2,128)} %pad_maximum_fusion.2), calls=%async_computation.6 | async-start | bytes 65536 | tf_op jit(solution)/shard_map/all_to_all | solution.py:133
  168.5 79.3 %reduce-scatter.6.cloned.1.call-start = ((), (), s32[]{:S(2)}) async-start(), calls=%async_computation.8 | async-start | bytes 1179648 | tf_op jit(solution)/shard_map/reduce_scatter | solution.py:161
  199.8 48.0 %copy-start.9 = (bf16[2,8,32,1024]{3,2,1,0:T(8,128)(2,1)S(1)}, bf16[2,8,32,1024]{3,2,1,0:T(8,128)(2,1)}, u32[]{:S(2)}) copy-start(bf16[2,8,32,1024]{3,2,1,0:T(8,128)(2,1)} %param.10) | copy-start | bytes 3145732
  201.8 45.9 %all-to-all-start.2 = ((bf16[2,256,1,1024]{3,0,2,1:T(2,128)(2,1)}), bf16[2,256,1,1024]{3,0,2,1:T(2,128)(2,1)}, u32[]{:S(2)}, u32[]{:S(2)}) async-start(bf16[2,256,1,1024]{3,0,2,1:T(2,128)(2,1)} %copy.131), calls=%async_computation.2 | async-start | bytes 2097152 | tf_op jit(solution)/shard_map/all_to_all | solution.py:124
  210.0 62.7 %reduce-scatter.8.cloned.1.call-start = ((), (), s32[]{:S(2)}) async-start(), calls=%async_computation.9 | async-start | bytes 163840 | tf_op jit(solution)/shard_map/reduce_scatter | solution.py:162
  247.8 42.2 %copy-start.1 = (bf16[1024,1024]{1,0:T(8,128)(2,1)S(1)}, bf16[1024,1024]{1,0:T(8,128)(2,1)}, u32[]{:S(2)}) copy-start(bf16[1024,1024]{1,0:T(8,128)(2,1)} %param.17) | copy-start | bytes 6291460
  (4 other events, 4.3 us)
Sparse Core Ops, SparseCore 0:
  153.2 45.7 reduce-scatter.3
  201.6 46.0 reduce-scatter.5
  250.2 22.4 reduce-scatter.7
